TPU v7x, 256 devices: a whole 4x4x8 slice. The times are simulated.
256 devices in a mesh: row: 16 (over z, x_lo), col: 4 (over x_hi, core), layer: 4 (over y).
Axes of the slice: x: 4 (x_hi: 2, x_lo: 2; x = x_hi * 2 + x_lo), y: 4, z: 8, core: 2. Of those that a mesh axis runs over, the one named last changes fastest.
Arguments:
- density: bfloat16 [512, 16, 128, 128], P('row', 'col'), may hold values from -0.59765625 to 0.59765625
- block_offset: int32 [512, 16], P('row', 'col'), may hold values from 0 to 1, as said below
- filter_offset: int32 [64, 32], P('row', 'col'), may hold values from 0 to 3, as said below
- position: int32 [32], replicated, may hold values from 0 to 31, each once
Outputs:
- purified: float32 [64, 32, 128, 128], P(('row', 'layer'), 'col')
Inputs may be any that keep to these rules, and one draw needn't show every extreme that they name: `block_offset`: slots fall into groups of 1 consecutive slots; within each group of a block row the offsets rise strictly (a group of one slot holds a single offset). `filter_offset`: slots fall into groups of 2 consecutive slots; within each group of a row the offsets rise strictly (a group of one slot holds a single offset).
All inputs are finite; a program needn't handle non-finite values.
Results may differ from a plain program's by a relative error of at most 0.0027.
Values may be sent and summed in bfloat16 or wider, within the bound.
No kernel may reach another device: no remote copies, remote signals or barrier semaphores. Data moves between devices by JAX's collectives and lax.ppermute only.
A program may use at most 128 MiB of HBM per device.

v0:
```python
import jax
import jax.numpy as jnp
from jax import lax
from jax.sharding import PartitionSpec as P

W = 16
WF = 32
RA = 4


def from_behind(value, axis, steps):
    count = lax.axis_size(axis)
    pairs = [(source, (source + steps) % count) for source in range(count)]
    return lax.ppermute(value, axis, pairs)


def column_index(offsets, local_rows, position, image_of, slot_base, group_size):
    extent = position.shape[0]
    groups = (slot_base + jnp.arange(offsets.shape[1], dtype=jnp.int32)) // group_size * extent
    physical = (position[local_rows][:, None] + offsets) % extent
    return groups[None, :] + image_of[physical]


def block_multiply(left_blocks, local_rows, right_blocks, right_columns, targets):
    picked = right_blocks[local_rows]
    picked_columns = right_columns[local_rows]
    matches = picked_columns[:, :, None, :] == targets[:, None, :, None]
    chosen = jnp.einsum(
        "nsut,nstyz->nsuyz",
        matches.astype(jnp.bfloat16),
        picked,
        preferred_element_type=jnp.float32,
    ).astype(jnp.bfloat16)
    return jnp.einsum("nsxy,nsuyz->nuxz", left_blocks, chosen, preferred_element_type=jnp.float32)


def on_device(density, block_offset, filter_offset, position):
    rows_tile = density.shape[0]
    slots_tile = density.shape[1]
    edge = density.shape[2]
    row_count = lax.axis_size("row")
    layer_count = lax.axis_size("layer")
    group_block = W // row_count
    group_filter = WF // row_count
    filter_slots = filter_offset.shape[1]
    row_id = lax.axis_index("row")
    col_id = lax.axis_index("col")
    layer_id = lax.axis_index("layer")
    extent = position.shape[0]
    image_of = jnp.zeros((extent,), jnp.int32).at[position].set(jnp.arange(extent, dtype=jnp.int32))
    right_columns = column_index(
        block_offset,
        jnp.arange(rows_tile, dtype=jnp.int32),
        position,
        image_of,
        col_id * slots_tile,
        group_block,
    )
    target_columns = column_index(
        filter_offset,
        jnp.arange(RA, dtype=jnp.int32),
        position,
        image_of,
        col_id * filter_slots,
        group_filter,
    )
    share_rows = RA // layer_count
    step_count = row_count // layer_count
    carried = (density, right_columns)
    for bit_number in range(layer_count.bit_length() - 1):
        moved = from_behind((carried[0], carried[1]), "row", step_count * (1 << bit_number))
        taken = layer_id >> bit_number & 1 == 1
        carried = (jnp.where(taken, moved[0], carried[0]), jnp.where(taken, moved[1], carried[1]))
    panels = []
    for turn_index in range(step_count):
        if turn_index > 0:
            carried = from_behind((carried[0], carried[1]), "row", 1)
        source = (row_id - layer_id * step_count - turn_index) % row_count
        panels.append((source, carried))

    def gather_left(left_blocks, left_columns):
        return (
            lax.all_gather(left_blocks, "col", axis=1, tiled=True),
            lax.all_gather(left_columns, "col", axis=1, tiled=True),
        )

    def panel_product(left_blocks, left_columns, group_size):
        full_blocks, full_columns = gather_left(left_blocks, left_columns)
        running = jnp.zeros((RA, filter_slots, edge, edge), jnp.float32)
        for source, received in panels:
            start = source * group_size
            piece = lax.dynamic_slice_in_dim(full_blocks, start, group_size, 1)
            piece_columns = lax.dynamic_slice_in_dim(full_columns, start, group_size, 1)
            running = running + block_multiply(
                piece, piece_columns - source * rows_tile, received[0], received[1], target_columns
            )
        return running

    square = panel_product(density[:RA], right_columns[:RA], group_block)
    summed = lax.psum(square, "layer")
    square_own = lax.dynamic_slice_in_dim(summed, layer_id * share_rows, share_rows, 0)
    square_half = summed.astype(jnp.bfloat16)
    cube = panel_product(square_half, target_columns, group_filter)
    cube_own = lax.psum_scatter(cube, "layer", scatter_dimension=0, tiled=True)
    return 3.0 * square_own - 2.0 * cube_own


def solution(mesh):
    placed = (P("row", "col", None, None), P("row", "col"), P("row", "col"), P())
    return jax.shard_map(
        on_device,
        mesh=mesh,
        in_specs=placed,
        out_specs=P(("row", "layer"), "col", None, None),
        check_vma=False,
    )
```

profile of v0, /device:TPU:1, one launch (start us, length us, event | category | flops | bytes accessed | tf_op | source)
XLA Modules:
  0.0 888.2 jit_solution(15324507685565275466)
XLA Ops:
  6.5 3.8 collective-permute-start.2
  10.3 130.0 %collective-permute-done.2 = bf16[32,4,128,128]{3,2,1,0:T(8,128)(2,1)} collective-permute-done((bf16[32,4,128,128]{3,2,1,0:T(8,128)(2,1)}, bf16[32,4,128,128]{3,2,1,0:T(8,128)(2,1)}, u32[]{:S(2)}, u32[]{:S(2)}) %collective-permute-start.2) | collective-permute-done | bytes 4194336 | tf_op jit(solution)/shard_map/ppermute | solution.py:14
  140.3 4.6 broadcast_select_fusion
  144.9 58.2 %collective-permute-start.3 = (bf16[32,4,128,128]{3,2,1,0:T(8,128)(2,1)}, bf16[32,4,128,128]{3,2,1,0:T(8,128)(2,1)}, u32[]{:S(2)}, u32[]{:S(2)}) collective-permute-start(bf16[32,4,128,128]{3,2,1,0:T(8,128)(2,1)} %broadcast_select_fusion), channel_id=1, source_target_pairs={{0,128},{16,144},{32,160},{48,176},{64,192},{80,208},{96,224},{112... | collective-permute-start | bytes 12582920 | tf_op jit(solution)/shard_map/ppermute | solution.py:14
  203.1 180.2 %collective-permute-done.3 = bf16[32,4,128,128]{3,2,1,0:T(8,128)(2,1)} collective-permute-done((bf16[32,4,128,128]{3,2,1,0:T(8,128)(2,1)}, bf16[32,4,128,128]{3,2,1,0:T(8,128)(2,1)}, u32[]{:S(2)}, u32[]{:S(2)}) %collective-permute-start.3) | collective-permute-done | bytes 4194336 | tf_op jit(solution)/shard_map/ppermute | solution.py:14
  383.3 2.6 broadcast_select_fusion.1
  389.1 92.5 %collective-permute-done.5 = bf16[32,4,128,128]{3,2,1,0:T(8,128)(2,1)} collective-permute-done((bf16[32,4,128,128]{3,2,1,0:T(8,128)(2,1)S(1)}, bf16[32,4,128,128]{3,2,1,0:T(8,128)(2,1)}, u32[]{:S(2)}, u32[]{:S(2)}) %collective-permute-start.5) | collective-permute-done | bytes 4194336 | tf_op jit(solution)/shard_map/ppermute | solution.py:14
  490.0 92.1 %collective-permute-done.7 = bf16[32,4,128,128]{3,2,1,0:T(8,128)(2,1)} collective-permute-done((bf16[32,4,128,128]{3,2,1,0:T(8,128)(2,1)}, bf16[32,4,128,128]{3,2,1,0:T(8,128)(2,1)}, u32[]{:S(2)}, u32[]{:S(2)}) %collective-permute-start.7) | collective-permute-done | bytes 4194336 | tf_op jit(solution)/shard_map/ppermute | solution.py:14
  585.2 94.4 %all-gather = s32[4,4,4]{2,1,0:T(4,128)S(1)} all-gather(s32[1,4,4]{2,1,0:T(4,128)S(1)} %bitcast.166), channel_id=1, replica_groups=mesh['row'=16,'col'=4,'layer'=4] {'col'}, dimensions={0}, use_global_device_ids=true | all-gather | bytes 320 | tf_op jit(solution)/shard_map/all_gather | solution.py:84
  680.4 5.3 collective-permute-start.1
  687.1 4.7 collective-permute-done.4
  691.8 4.7 collective-permute-done.6
  698.2 3.0 collective-permute-done.8
  701.8 2.8 gather_fusion.5
  706.7 2.8 gather_fusion.7
  710.2 2.8 fusion.18
  713.0 2.8 gather_fusion.9
  716.5 2.8 fusion.16
  719.2 2.8 gather_fusion.11
  722.7 4.2 add_bitcast_fusion
  727.0 66.7 %all-reduce.2.cloned.1.call-done = f32[4,8,128,128]{2,3,1,0:T(8,128)} async-done(((f32[4,8,128,128]{2,3,1,0:T(8,128)}), f32[4,8,128,128]{2,3,1,0:T(8,128)}) %all-reduce.2.cloned.1.call-update) | async-done | bytes 2097168 | tf_op jit(solution)/shard_map/psum | solution.py:100
  793.7 2.7 convert_element_type.44
  796.6 7.6 all-gather.1
  806.9 3.3 gather_fusion.13
  812.5 2.9 gather_fusion.15
  816.7 3.0 gather_fusion.17
  819.6 2.2 convolution_convert_fusion.1
  821.9 3.0 gather_fusion.19
  827.1 10.9 %all-gather.7.cloned.1.call-done = bf16[4,32,128,128]{2,3,1,0:T(8,128)(2,1)} async-done(((bf16[4,8,128,128]{2,3,1,0:T(8,128)(2,1)}), bf16[4,32,128,128]{2,3,1,0:T(8,128)(2,1)}) %all-gather.7.cloned.1.call-update) | async-done | bytes 4194320 | tf_op jit(solution)/shard_map/all_gather | solution.py:83
  838.0 2.7 fusion.1
  844.6 3.3 fusion
  848.0 31.4 %reduce-scatter.2.cloned.1.call-done = f32[1,8,128,128]{2,3,1,0:T(8,128)} async-done(((f32[4,8,128,128]{2,3,1,0:T(8,128)}), f32[1,8,128,128]{2,3,1,0:T(8,128)}) %reduce-scatter.2.cloned.1.call-update) | async-done | bytes 524304 | tf_op jit(solution)/shard_map/reduce_scatter | solution.py:104
  (107 shorter events, 37.6 us)
Async XLA Ops:
  6.5 698.7 %all-gather.5.cloned.1.call-start = ((), (), s32[]{:S(2)}) async-start(), calls=%async_computation.1 | async-start | bytes 2621440 | tf_op jit(solution)/shard_map/all_gather | solution.py:83
  6.5 133.8 %collective-permute-start.2 = (bf16[32,4,128,128]{3,2,1,0:T(8,128)(2,1)}, bf16[32,4,128,128]{3,2,1,0:T(8,128)(2,1)}, u32[]{:S(2)}, u32[]{:S(2)}) collective-permute-start(bf16[32,4,128,128]{3,2,1,0:T(8,128)(2,1)} %param.4), channel_id=1, source_target_pairs={{0,64},{16,80},{32,96},{48,112},{64,128},{80,144},{96,160},{112,17... | collective-permute-start | bytes 12582920 | tf_op jit(solution)/shard_map/ppermute | solution.py:14
  144.9 238.4 %collective-permute-start.3 = (bf16[32,4,128,128]{3,2,1,0:T(8,128)(2,1)}, bf16[32,4,128,128]{3,2,1,0:T(8,128)(2,1)}, u32[]{:S(2)}, u32[]{:S(2)}) collective-permute-start(bf16[32,4,128,128]{3,2,1,0:T(8,128)(2,1)} %broadcast_select_fusion), channel_id=1, source_target_pairs={{0,128},{16,144},{32,160},{48,176},{64,192},{80,208},{96,224},{112... | collective-permute-start | bytes 12582920 | tf_op jit(solution)/shard_map/ppermute | solution.py:14
  203.1 278.9 %copy-start = (s32[32]{0:T(128)S(1)}, s32[32]{0:T(128)}, u32[]{:S(2)}) copy-start(s32[32]{0:T(128)} %param.7) | copy-start | bytes 388
  203.1 279.6 %copy-start.4 = (s32[32,4]{0,1:T(4,128)S(1)}, s32[32,4]{0,1:T(4,128)}, u32[]{:S(2)}) copy-start(s32[32,4]{0,1:T(4,128)} %param.5) | copy-start | bytes 1540
  385.9 2.0 copy-start.3
  387.9 93.8 %collective-permute-start.5 = (bf16[32,4,128,128]{3,2,1,0:T(8,128)(2,1)S(1)}, bf16[32,4,128,128]{3,2,1,0:T(8,128)(2,1)}, u32[]{:S(2)}, u32[]{:S(2)}) collective-permute-start(bf16[32,4,128,128]{3,2,1,0:T(8,128)(2,1)S(1)} %broadcast_select_fusion.1), channel_id=1, source_target_pairs={{0,16},{16,32},{32,48},{48,64},{64,80},{80,96},{96,112},{112,128},... | collective-permute-start | bytes 12582920 | tf_op jit(solution)/shard_map/ppermute | solution.py:14
  481.6 100.5 %collective-permute-start.7 = (bf16[32,4,128,128]{3,2,1,0:T(8,128)(2,1)}, bf16[32,4,128,128]{3,2,1,0:T(8,128)(2,1)}, u32[]{:S(2)}, u32[]{:S(2)}) collective-permute-start(bf16[32,4,128,128]{3,2,1,0:T(8,128)(2,1)} %collective-permute-done.5), channel_id=1, source_target_pairs={{0,16},{16,32},{32,48},{48,64},{64,80},{80,96},{96,112},{112,128},... | collective-permute-start | bytes 12582920 | tf_op jit(solution)/shard_map/ppermute | solution.py:14
  484.9 4.9 copy-start.5
  485.0 195.3 %collective-permute-start = (s32[32,4]{1,0:T(8,128)S(1)}, s32[32,4]{1,0:T(8,128)S(1)}, u32[]{:S(2)}, u32[]{:S(2)}) collective-permute-start(s32[32,4]{1,0:T(8,128)S(1)} %broadcast_add_fusion), channel_id=1, source_target_pairs={{0,64},{16,80},{32,96},{48,112},{64,128},{80,144},{96,160},{112,17... | collective-permute-start | bytes 1544 | tf_op jit(solution)/shard_map/ppermute | solution.py:14
  489.1 304.6 %all-reduce.2.cloned.1.call-start = ((), (), s32[]{:S(2)}) async-start(), calls=%async_computation.2 | async-start | bytes 4194304 | tf_op jit(solution)/shard_map/psum | solution.py:100
  582.1 137.1 %collective-permute-start.9 = (bf16[32,4,128,128]{3,2,1,0:T(8,128)(2,1)}, bf16[32,4,128,128]{3,2,1,0:T(8,128)(2,1)}, u32[]{:S(2)}, u32[]{:S(2)}) collective-permute-start(bf16[32,4,128,128]{3,2,1,0:T(8,128)(2,1)} %collective-permute-done.7), channel_id=1, source_target_pairs={{0,16},{16,32},{32,48},{48,64},{64,80},{80,96},{96,112},{112,128},... | collective-permute-start | bytes 12582920 | tf_op jit(solution)/shard_map/ppermute | solution.py:14
  680.4 6.7 collective-permute-start.1
  687.1 4.7 collective-permute-start.4
  691.8 4.7 collective-permute-start.6
  696.5 4.7 collective-permute-start.8
  727.0 111.1 %all-gather.7.cloned.1.call-start = ((), (), s32[]{:S(2)}) async-start(), calls=%async_computation.3 | async-start | bytes 5242880 | tf_op jit(solution)/shard_map/all_gather | solution.py:83
  796.5 82.9 %reduce-scatter.2.cloned.1.call-start = ((), (), s32[]{:S(2)}) async-start(), calls=%async_computation.4 | async-start | bytes 2621440 | tf_op jit(solution)/shard_map/reduce_scatter | solution.py:104
  838.0 2.7 copy-start.1
  842.6 2.0 copy-start.2
Sparse Core Ops, SparseCore 0:
  489.2 41.7 all-gather.4
  727.1 66.5 all-reduce.1
  796.6 41.3 all-gather.6
  848.1 31.2 reduce-scatter.1
where the time goes:
time: 889 us; the launch traced here: 888 us
  waiting for transfers between devices  618 us (70%)
  blocking collectives  102 us (11%)
  starting transfers between devices  73.4 us (8%)
  local copies, waits for them, and re-layouts  38.1 us (4%)
  matrix products  31.5 us (4%)
  between operations  13.6 us (2%)
  other arithmetic  11.8 us (1%)
    ppermute x10, waiting for transfers between devices, from_behind(): return lax.ppermute(value, axis, pairs)  509 us
    all_gather x2, blocking collectives, gather_left(): lax.all_gather(left_columns, 'col', axis=1, tiled=True)  102 us
    ppermute x10, starting transfers between devices, from_behind(): return lax.ppermute(value, axis, pairs)  73.2 us
    psum x1, waiting for transfers between devices, on_device(): summed = lax.psum(square, 'layer')  66.7 us
    reduce_scatter x1, waiting for transfers between devices, on_device(): cube_own = lax.psum_scatter(cube, 'layer', scatter_dimension=0, tiled=True)  31.4 us
    gather x8, local copies, waits for them, and re-layouts, block_multiply(): picked = right_blocks[local_rows]  23.5 us
    dot_general x8, matrix products, block_multiply(): jnp.einsum('nsxy,nsuyz->nuxz', left_blocks, chosen, preferred_element_typ...  21.1 us
  transfers between devices with their start and end apart: 14, of which 11 were waited for; matrix products, arithmetic and copies ran while one was open for 6% of the time, Pallas kernels for 0%

commit v1 on v0

--- a/solution.py
+++ b/solution.py
@@ -1,11 +1,20 @@
+import functools
 import jax
 import jax.numpy as jnp
 from jax import lax
 from jax.sharding import PartitionSpec as P
+from jax.lax import all_gather
 
 W = 16
 WF = 32
 RA = 4
+
+
+def watch_object_now(vals, row_axis):
+    return all_gather(vals, axis_name=row_axis).sum(axis=0)
+
+
+_rest_tracks = functools.partial(watch_object_now, row_axis="layer")
 
 
 def from_behind(value, axis, steps):
@@ -97,7 +106,7 @@
         return running
 
     square = panel_product(density[:RA], right_columns[:RA], group_block)
-    summed = lax.psum(square, "layer")
+    summed = _rest_tracks(square)
     square_own = lax.dynamic_slice_in_dim(summed, layer_id * share_rows, share_rows, 0)
     square_half = summed.astype(jnp.bfloat16)
     cube = panel_product(square_half, target_columns, group_filter)

time: 889 us -> 918 us (1.033)
  waiting for transfers between devices: 618 us -> 640 us
    all_gather x0 -> x1, waiting for transfers between devices: none -> 88.5 us  [watch_object_now(): return all_gather(vals, axis_name=row_axis).sum(axis=0)]
    psum x1 -> x0, waiting for transfers between devices: 66.7 us -> none  [on_device(): summed = lax.psum(square, 'layer')]
where the time goes in v1:
time: 918 us; the launch traced here: 917 us
  waiting for transfers between devices  640 us (70%)
  blocking collectives  102 us (11%)
  starting transfers between devices  73.4 us (8%)
  local copies, waits for them, and re-layouts  41.1 us (4%)
  matrix products  32.7 us (4%)
  other arithmetic  14.6 us (2%)
  between operations  13.6 us (1%)
    ppermute x10, waiting for transfers between devices, from_behind(): return lax.ppermute(value, axis, pairs)  509 us
    all_gather x2, blocking collectives, gather_left(): lax.all_gather(left_columns, 'col', axis=1, tiled=True)  102 us
    all_gather x1, waiting for transfers between devices, watch_object_now(): return all_gather(vals, axis_name=row_axis).sum(axis=0)  88.5 us
    ppermute x10, starting transfers between devices, from_behind(): return lax.ppermute(value, axis, pairs)  73.2 us
    reduce_scatter x1, waiting for transfers between devices, on_device(): cube_own = lax.psum_scatter(cube, 'layer', scatter_dimension=0, tiled=True)  31.2 us
    gather x8, local copies, waits for them, and re-layouts, block_multiply(): picked = right_blocks[local_rows]  23.4 us
    dot_general x8, matrix products, block_multiply(): jnp.einsum('nsxy,nsuyz->nuxz', left_blocks, chosen, preferred_element_typ...  21.2 us
  transfers between devices with their start and end apart: 14, of which 11 were waited for; matrix products, arithmetic and copies ran while one was open for 6% of the time, Pallas kernels for 0%

profile of v1, /device:TPU:1, one launch (start us, length us, event | category | flops | bytes accessed | tf_op | source)
XLA Modules:
  0.0 917.1 jit_solution(1635960470194171062)
XLA Ops:
  6.5 3.8 collective-permute-start.2
  10.3 130.0 %collective-permute-done.2 = bf16[32,4,128,128]{3,2,1,0:T(8,128)(2,1)} collective-permute-done((bf16[32,4,128,128]{3,2,1,0:T(8,128)(2,1)}, bf16[32,4,128,128]{3,2,1,0:T(8,128)(2,1)}, u32[]{:S(2)}, u32[]{:S(2)}) %collective-permute-start.2) | collective-permute-done | bytes 4194336 | tf_op jit(solution)/shard_map/ppermute | solution.py:23
  140.3 4.6 broadcast_select_fusion
  144.9 58.2 %collective-permute-start.3 = (bf16[32,4,128,128]{3,2,1,0:T(8,128)(2,1)}, bf16[32,4,128,128]{3,2,1,0:T(8,128)(2,1)}, u32[]{:S(2)}, u32[]{:S(2)}) collective-permute-start(bf16[32,4,128,128]{3,2,1,0:T(8,128)(2,1)} %broadcast_select_fusion), channel_id=1, source_target_pairs={{0,128},{16,144},{32,160},{48,176},{64,192},{80,208},{96,224},{112... | collective-permute-start | bytes 12582920 | tf_op jit(solution)/shard_map/ppermute | solution.py:23
  203.1 180.2 %collective-permute-done.3 = bf16[32,4,128,128]{3,2,1,0:T(8,128)(2,1)} collective-permute-done((bf16[32,4,128,128]{3,2,1,0:T(8,128)(2,1)}, bf16[32,4,128,128]{3,2,1,0:T(8,128)(2,1)}, u32[]{:S(2)}, u32[]{:S(2)}) %collective-permute-start.3) | collective-permute-done | bytes 4194336 | tf_op jit(solution)/shard_map/ppermute | solution.py:23
  383.3 2.6 broadcast_select_fusion.1
  389.1 92.5 %collective-permute-done.5 = bf16[32,4,128,128]{3,2,1,0:T(8,128)(2,1)} collective-permute-done((bf16[32,4,128,128]{3,2,1,0:T(8,128)(2,1)S(1)}, bf16[32,4,128,128]{3,2,1,0:T(8,128)(2,1)}, u32[]{:S(2)}, u32[]{:S(2)}) %collective-permute-start.5) | collective-permute-done | bytes 4194336 | tf_op jit(solution)/shard_map/ppermute | solution.py:23
  490.0 92.1 %collective-permute-done.7 = bf16[32,4,128,128]{3,2,1,0:T(8,128)(2,1)} collective-permute-done((bf16[32,4,128,128]{3,2,1,0:T(8,128)(2,1)}, bf16[32,4,128,128]{3,2,1,0:T(8,128)(2,1)}, u32[]{:S(2)}, u32[]{:S(2)}) %collective-permute-start.7) | collective-permute-done | bytes 4194336 | tf_op jit(solution)/shard_map/ppermute | solution.py:23
  585.2 94.4 %all-gather.1 = s32[4,4,4]{2,1,0:T(4,128)S(1)} all-gather(s32[1,4,4]{2,1,0:T(4,128)S(1)} %bitcast.168), channel_id=1, replica_groups=mesh['row'=16,'col'=4,'layer'=4] {'col'}, dimensions={0}, use_global_device_ids=true | all-gather | bytes 320 | tf_op jit(solution)/shard_map/all_gather | solution.py:93
  680.4 5.3 collective-permute-start.1
  687.1 4.7 collective-permute-done.4
  691.8 4.7 collective-permute-done.6
  698.2 3.0 collective-permute-done.8
  701.8 2.8 gather_fusion.5
  706.7 2.8 gather_fusion.7
  710.2 2.8 fusion.18
  713.0 2.8 gather_fusion.9
  716.5 2.8 fusion.16
  719.2 2.8 gather_fusion.11
  722.7 4.2 add_bitcast_fusion
  727.0 2.9 copy.32
  730.0 88.5 %all-gather.11.cloned.1.call-done = f32[16,8,128,128]{3,2,1,0:T(8,128)} async-done(((f32[4,8,128,128]{3,2,1,0:T(8,128)}), f32[16,8,128,128]{3,2,1,0:T(8,128)}) %all-gather.11.cloned.1.call-update) | async-done | bytes 8388624 | tf_op jit(solution)/shard_map/all_gather | solution.py:14
  818.5 4.4 reduce_sum.9
  824.3 7.6 all-gather.2
  834.7 3.0 gather_fusion.13
  839.9 3.1 gather_fusion.15
  845.2 3.0 gather_fusion.17
  850.5 3.0 gather_fusion.19
  855.6 11.3 %all-gather.9.cloned.1.call-done = bf16[4,32,128,128]{3,2,1,0:T(8,128)(2,1)} async-done(((bf16[4,8,128,128]{3,2,1,0:T(8,128)(2,1)}), bf16[4,32,128,128]{3,2,1,0:T(8,128)(2,1)}) %all-gather.9.cloned.1.call-update) | async-done | bytes 4194320 | tf_op jit(solution)/shard_map/all_gather | solution.py:92
  866.9 2.7 fusion.3
  873.7 3.3 fusion
  877.3 31.2 %reduce-scatter.2.cloned.1.call-done = f32[1,8,128,128]{2,3,1,0:T(8,128)} async-done(((f32[4,8,128,128]{2,3,1,0:T(8,128)}), f32[1,8,128,128]{2,3,1,0:T(8,128)}) %reduce-scatter.2.cloned.1.call-update) | async-done | bytes 524304 | tf_op jit(solution)/shard_map/reduce_scatter | solution.py:113
  (113 shorter events, 42.3 us)
Async XLA Ops:
  6.5 698.7 %all-gather.7.cloned.1.call-start = ((), (), s32[]{:S(2)}) async-start(), calls=%async_computation.1 | async-start | bytes 2621440 | tf_op jit(solution)/shard_map/all_gather | solution.py:92
  6.5 133.8 %collective-permute-start.2 = (bf16[32,4,128,128]{3,2,1,0:T(8,128)(2,1)}, bf16[32,4,128,128]{3,2,1,0:T(8,128)(2,1)}, u32[]{:S(2)}, u32[]{:S(2)}) collective-permute-start(bf16[32,4,128,128]{3,2,1,0:T(8,128)(2,1)} %param.4), channel_id=1, source_target_pairs={{0,64},{16,80},{32,96},{48,112},{64,128},{80,144},{96,160},{112,17... | collective-permute-start | bytes 12582920 | tf_op jit(solution)/shard_map/ppermute | solution.py:23
  144.9 238.4 %collective-permute-start.3 = (bf16[32,4,128,128]{3,2,1,0:T(8,128)(2,1)}, bf16[32,4,128,128]{3,2,1,0:T(8,128)(2,1)}, u32[]{:S(2)}, u32[]{:S(2)}) collective-permute-start(bf16[32,4,128,128]{3,2,1,0:T(8,128)(2,1)} %broadcast_select_fusion), channel_id=1, source_target_pairs={{0,128},{16,144},{32,160},{48,176},{64,192},{80,208},{96,224},{112... | collective-permute-start | bytes 12582920 | tf_op jit(solution)/shard_map/ppermute | solution.py:23
  203.1 279.0 %copy-start = (s32[32]{0:T(128)S(1)}, s32[32]{0:T(128)}, u32[]{:S(2)}) copy-start(s32[32]{0:T(128)} %param.7) | copy-start | bytes 388
  203.1 279.7 %copy-start.5 = (s32[32,4]{0,1:T(4,128)S(1)}, s32[32,4]{0,1:T(4,128)}, u32[]{:S(2)}) copy-start(s32[32,4]{0,1:T(4,128)} %param.5) | copy-start | bytes 1540
  385.9 2.0 copy-start.4
  387.9 93.8 %collective-permute-start.5 = (bf16[32,4,128,128]{3,2,1,0:T(8,128)(2,1)S(1)}, bf16[32,4,128,128]{3,2,1,0:T(8,128)(2,1)}, u32[]{:S(2)}, u32[]{:S(2)}) collective-permute-start(bf16[32,4,128,128]{3,2,1,0:T(8,128)(2,1)S(1)} %broadcast_select_fusion.1), channel_id=1, source_target_pairs={{0,16},{16,32},{32,48},{48,64},{64,80},{80,96},{96,112},{112,128},... | collective-permute-start | bytes 12582920 | tf_op jit(solution)/shard_map/ppermute | solution.py:23
  481.6 100.5 %collective-permute-start.7 = (bf16[32,4,128,128]{3,2,1,0:T(8,128)(2,1)}, bf16[32,4,128,128]{3,2,1,0:T(8,128)(2,1)}, u32[]{:S(2)}, u32[]{:S(2)}) collective-permute-start(bf16[32,4,128,128]{3,2,1,0:T(8,128)(2,1)} %collective-permute-done.5), channel_id=1, source_target_pairs={{0,16},{16,32},{32,48},{48,64},{64,80},{80,96},{96,112},{112,128},... | collective-permute-start | bytes 12582920 | tf_op jit(solution)/shard_map/ppermute | solution.py:23
  484.9 4.9 copy-start.6
  485.1 195.3 %collective-permute-start = (s32[32,4]{1,0:T(8,128)S(1)}, s32[32,4]{1,0:T(8,128)S(1)}, u32[]{:S(2)}, u32[]{:S(2)}) collective-permute-start(s32[32,4]{1,0:T(8,128)S(1)} %broadcast_add_fusion), channel_id=1, source_target_pairs={{0,64},{16,80},{32,96},{48,112},{64,128},{80,144},{96,160},{112,17... | collective-permute-start | bytes 1544 | tf_op jit(solution)/shard_map/ppermute | solution.py:23
  489.1 329.4 %all-gather.11.cloned.1.call-start = ((), (), s32[]{:S(2)}) async-start(), calls=%async_computation.4 | async-start | bytes 10485760 | tf_op jit(solution)/shard_map/all_gather | solution.py:14
  582.1 137.1 %collective-permute-start.9 = (bf16[32,4,128,128]{3,2,1,0:T(8,128)(2,1)}, bf16[32,4,128,128]{3,2,1,0:T(8,128)(2,1)}, u32[]{:S(2)}, u32[]{:S(2)}) collective-permute-start(bf16[32,4,128,128]{3,2,1,0:T(8,128)(2,1)} %collective-permute-done.7), channel_id=1, source_target_pairs={{0,16},{16,32},{32,48},{48,64},{64,80},{80,96},{96,112},{112,128},... | collective-permute-start | bytes 12582920 | tf_op jit(solution)/shard_map/ppermute | solution.py:23
  680.4 6.7 collective-permute-start.1
  687.1 4.7 collective-permute-start.4
  691.8 4.7 collective-permute-start.6
  696.5 4.7 collective-permute-start.8
  729.9 137.0 %all-gather.9.cloned.1.call-start = ((), (), s32[]{:S(2)}) async-start(), calls=%async_computation.2 | async-start | bytes 5242880 | tf_op jit(solution)/shard_map/all_gather | solution.py:92
  824.2 84.3 %reduce-scatter.2.cloned.1.call-start = ((), (), s32[]{:S(2)}) async-start(), calls=%async_computation.3 | async-start | bytes 2621440 | tf_op jit(solution)/shard_map/reduce_scatter | solution.py:113
  866.9 2.7 copy-start.1
  869.6 2.0 copy-start.2
  871.6 2.0 copy-start.3
Sparse Core Ops, SparseCore 0:
  489.2 41.7 all-gather.6
  730.0 88.4 all-gather.10
  824.3 42.5 all-gather.8
  877.1 31.2 reduce-scatter.1
